TPU v7x, 256 devices: a whole 4x4x8 slice. The times are simulated.
256 devices in a mesh: slab: 32 (over z, x), coil: 8 (over y, core).
Axes of the slice: x: 4, y: 4, z: 8, core: 2. Of those that a mesh axis runs over, the one named last changes fastest.
Arguments:
- noisy: float32 [2, 64, 256, 128], P(None, 'slab', 'coil'), may hold values from -6 to 6
- step_index: int32 [], replicated, may hold values from 200 to 599
- w_in: bfloat16 [3, 3, 3, 32, 2], replicated, may hold values from -0.875 to 0.875
- w_mid: bfloat16 [3, 3, 3, 32, 32], replicated, may hold values from -0.21875 to 0.21875
- w_out: bfloat16 [3, 3, 3, 2, 32], replicated, may hold values from -0.21875 to 0.21875
- time_weight: float32 [32, 32], replicated, may hold values from -1 to 1
- sens: float32 [16, 2, 64, 256, 128], P('coil', None, 'slab')
- kdata: float32 [16, 2, 64, 256, 128], P('coil', None, None, 'slab'), may hold values from -4 to 4
- mask: int32 [64, 256], P(None, 'slab'), may hold values from 0 to 1, as said below
Outputs:
- recon: float32 [2, 64, 256, 128], P(None, 'slab', 'coil')
- next_sample: float32 [2, 64, 256, 128], P(None, 'slab', 'coil')
Inputs may be any that keep to these rules, and one draw needn't show every extreme that they name: mask[kz, ky] is 1 wherever min(kz, 64 - kz) < max(1, 4) and min(ky, 256 - ky) < max(1, 8); every other entry is 1 with chance one in three.
All inputs are finite; a program needn't handle non-finite values.
Results may differ from a plain program's by a relative error of at most 0.0023.
Values may be sent and summed in bfloat16 or wider, within the bound.
No kernel may reach another device: no remote copies, remote signals or barrier semaphores. Data moves between devices by JAX's collectives and lax.ppermute only.
A program may use at most 64 MiB of HBM per device.

v0:
```python
import math
import jax
import jax.numpy as jnp
from jax import lax
from jax.sharding import PartitionSpec as P

ITERS = 2
STEPS = 1000
STRIDE = 20
REG_WEIGHT = 0.5
HIGHEST_PRECISION = lax.Precision.HIGHEST


def extended(cells, sides, width):
    for axis, dim in sides:
        count = lax.axis_size(axis)
        ends = count - 1
        head = lax.slice_in_dim(cells, 0, width, axis=dim)
        tail = lax.slice_in_dim(cells, cells.shape[dim] - width, cells.shape[dim], axis=dim)
        cells = jnp.concatenate(
            [
                lax.ppermute(tail, axis, [(i, (i + 1) % count) for i in range(ends)]),
                cells,
                lax.ppermute(head, axis, [((i + 1) % count, i) for i in range(ends)]),
            ],
            axis=dim,
        )
    return cells


def plan_level(step_value):
    angle = (step_value / STEPS + 0.008) / 1.008 * (math.pi / 2)
    return jnp.cos(angle) ** 2


def time_bias(step_value, time_weight):
    half = time_weight.shape[0] // 2
    freqs = jnp.exp(-math.log(10000.0) * jnp.arange(half, dtype=jnp.float32) / half)
    phase = step_value * freqs
    embed = jnp.concatenate([jnp.sin(phase), jnp.cos(phase)])
    return jnp.dot(embed, time_weight, precision=HIGHEST_PRECISION)


def conv_layer(inputs, weights):
    padded = extended(inputs, (("slab", 1), ("coil", 2)), 1)
    kernel = jnp.transpose(weights, (3, 4, 0, 1, 2))
    result = lax.conv_general_dilated(
        padded[None],
        kernel,
        (1, 1, 1),
        ((0, 0), (0, 0), (1, 1)),
        dimension_numbers=("NCDHW", "OIDHW", "NCDHW"),
        preferred_element_type=jnp.float32,
    )
    return result[0]


def dft_blocks(length, inverse):
    index = jnp.arange(length, dtype=jnp.int32)
    product = index[:, None] * index[None, :] % length
    theta = product.astype(jnp.float32) * (2.0 * math.pi / length)
    cosine = jnp.cos(theta) / math.sqrt(length)
    sine = jnp.sin(theta) / math.sqrt(length)
    if inverse:
        sine = -sine
    upper = jnp.stack([cosine, sine], axis=1)
    lower = jnp.stack([-sine, cosine], axis=1)
    return jnp.stack([upper, lower], axis=0)


def along_last(data, blocks):
    return jnp.einsum("pkqn,cqzyn->cpzyk", blocks, data, precision=HIGHEST_PRECISION)


def along_rows(data, blocks):
    return jnp.einsum("pkqn,cqzny->cpzky", blocks, data, precision=HIGHEST_PRECISION)


def along_depth(data, blocks):
    return jnp.einsum("pkqn,cqnyx->cpkyx", blocks, data, precision=HIGHEST_PRECISION)


def times_sens(sens, image):
    real_part = sens[:, 0] * image[0] - sens[:, 1] * image[1]
    imag_part = sens[:, 0] * image[1] + sens[:, 1] * image[0]
    return jnp.stack([real_part, imag_part], axis=1)


def times_conj(sens, images):
    real_part = jnp.sum(sens[:, 0] * images[:, 0] + sens[:, 1] * images[:, 1], axis=0)
    imag_part = jnp.sum(sens[:, 0] * images[:, 1] - sens[:, 1] * images[:, 0], axis=0)
    return jnp.stack([real_part, imag_part])


def coil_term(image_full, sens, kdata_x, weight, blocks, with_data):
    forward_y, forward_z, inverse_y, inverse_z = blocks
    coil_images = times_sens(sens, image_full)
    spectrum = along_rows(coil_images, forward_y)
    pencils = lax.all_to_all(
        spectrum.astype(jnp.bfloat16), "slab", split_axis=3, concat_axis=2, tiled=True
    ).astype(jnp.float32)
    kspace = along_depth(pencils, forward_z)
    if with_data:
        kspace = weight * (kdata_x - kspace)
    else:
        kspace = weight * kspace
    back = along_depth(kspace, inverse_z)
    slabs = lax.all_to_all(
        back.astype(jnp.bfloat16), "slab", split_axis=2, concat_axis=3, tiled=True
    ).astype(jnp.float32)
    images = along_rows(slabs, inverse_y)
    return times_conj(sens, images)


def combine_coils(partial_value):
    count = lax.axis_size("coil")
    pieces = lax.all_to_all(partial_value, "coil", split_axis=2, concat_axis=0, tiled=True)
    pieces = pieces.reshape((count, partial_value.shape[0]) + pieces.shape[1:])
    return jnp.sum(pieces, axis=0)


def gather_rows(value):
    return lax.all_gather(value, "coil", axis=2, tiled=True)


def global_sums(values):
    axes = ("slab", "coil")
    count = lax.axis_size("slab") * lax.axis_size("coil")
    spread = jnp.broadcast_to(values[None], (count,) + values.shape)
    return jnp.sum(lax.all_to_all(spread, axes, split_axis=0, concat_axis=0, tiled=True), axis=0)


def body(noisy, step_index, w_in, w_mid, w_out, time_weight, sens, kdata, mask):
    step_value = step_index.astype(jnp.float32)
    signal_level = plan_level(step_value)
    prior_level = plan_level(step_value - STRIDE)
    bias = time_bias(step_value, time_weight)
    hidden = jax.nn.silu(
        conv_layer(noisy.astype(jnp.bfloat16), w_in) + bias[:, None, None, None]
    ).astype(jnp.bfloat16)
    mixed = (hidden.astype(jnp.float32) + jax.nn.silu(conv_layer(hidden, w_mid))).astype(
        jnp.bfloat16
    )
    noise_pred = conv_layer(mixed, w_out)
    estimate = (noisy - jnp.sqrt(1.0 - signal_level) * noise_pred) / jnp.sqrt(signal_level)
    depth_full = kdata.shape[2]
    rows_full = sens.shape[3]
    width = sens.shape[4]
    blocks = (
        dft_blocks(rows_full, False),
        dft_blocks(depth_full, False),
        dft_blocks(rows_full, True),
        dft_blocks(depth_full, True),
    )
    kdata_x = along_last(kdata, dft_blocks(width, True))
    weight = mask.astype(jnp.float32)[None, None, :, :, None]

    def operator(image, with_data):
        return combine_coils(
            coil_term(gather_rows(image), sens, kdata_x, weight, blocks, with_data)
        )

    solution = estimate
    residual = operator(estimate, True)
    direction = residual
    norm_now = None
    for iteration in range(ITERS):
        final_turn = iteration + 1 == ITERS
        image = operator(direction, False) + REG_WEIGHT * direction
        if norm_now is None:
            sums = global_sums(
                jnp.stack([jnp.sum(residual * residual), jnp.sum(direction * image)])
            )
            norm_now, curvature = (sums[0], sums[1])
        else:
            curvature = global_sums(jnp.stack([jnp.sum(direction * image)]))[0]
        step_size = norm_now / curvature
        solution = solution + step_size * direction
        if not final_turn:
            residual = residual - step_size * image
            norm_next = global_sums(jnp.stack([jnp.sum(residual * residual)]))[0]
            direction = residual + norm_next / norm_now * direction
            norm_now = norm_next
    recon = solution
    next_sample = jnp.sqrt(prior_level) * recon + jnp.sqrt(1.0 - prior_level) * noise_pred
    return (recon, next_sample)


def solution(mesh):
    return jax.shard_map(
        body,
        mesh=mesh,
        in_specs=(
            P(None, "slab", "coil", None),
            P(),
            P(),
            P(),
            P(),
            P(),
            P("coil", None, "slab", None, None),
            P("coil", None, None, "slab", None),
            P(None, "slab"),
        ),
        out_specs=(P(None, "slab", "coil", None), P(None, "slab", "coil", None)),
        check_vma=False,
    )
```

profile of v0, /device:TPU:1, one launch (start us, length us, event | category | flops | bytes accessed | tf_op | source)
XLA Modules:
  0.0 684.9 jit_solution(6342718819612224770)
XLA Ops:
  10.0 5.2 collective-permute-start.2
  22.7 7.8 %broadcast_select_fusion.1 = f32[2,32,8,17,32]{4,2,3,1,0:T(8,128)S(1)} fusion(pred[8,17]{0,1:T(8,128)(4,1)} %constant.113, bf16[3,3,3,32,2]{3,4,2,1,0:T(2,128)(2,1)} %param.11, bf16[2,4,34,1,7,2]{4,0,5,2,1,3:T(2,128)(2,1)S(1)} %slice.155, bf16[2,4,34,1,8,17]{4,0,5,2,1,3:T(2,128)(2,1)S(1)} %copy.378), kind=kOutput, calls=%fused_computation.23 | convolution fusion | flops 30607616 | bytes 1199304 | tf_op jit(solution)/shard_map/conv_general_dilated | solution.py:47
  36.8 4.1 collective-permute-start.4
  70.6 4.6 maximum_bitcast_fusion
  75.3 8.1 %copy.497 = bf16[32,4,34,1,128]{2,0,4,1,3:T(8,128)(2,1)} copy(bf16[32,4,34,1,128]{0,2,4,1,3:T(8,128)(2,1)} %maximum_bitcast_fusion) | data formatting | bytes 2228224
  83.3 5.2 pad.2.clone
  88.5 8.7 %copy.386 = bf16[32,4,34,1,8,17]{0,4,5,2,1,3:T(8,128)(2,1)} copy(bf16[32,4,34,1,8,17]{2,0,5,4,1,3:T(8,128)(2,1)} %bitcast.328) | data formatting | bytes 2367488 | tf_op jit(solution)/shard_map/conv_general_dilated | solution.py:47
  98.5 8.6 %broadcast_select_fusion = f32[2,32,8,17,32]{4,2,3,1,0:T(8,128)S(1)} fusion(pred[8,17]{0,1:T(8,128)(4,1)S(1)} %copy-done.25, bf16[3,3,3,32,32]{4,3,2,1,0:T(8,128)(2,1)S(1)} %copy-done.26, bf16[32,4,34,1,7,2]{0,4,5,2,1,3:T(8,128)(2,1)S(1)} %slice.159, bf16[32,4,34,1,8,17]{0,4,5,2,1,3:T(8,128)(2,1)} %copy.386), kind=kOutput, calls=%fused_computation.22 | convolution fusion | flops 485543936 | bytes 2475144 | tf_op jit(solution)/shard_map/conv_general_dilated | solution.py:47
  115.4 4.5 collective-permute-start.8
  137.0 5.1 collective-permute-start.10
  150.1 6.3 maximum_bitcast_fusion.1
  156.4 8.1 %copy.498 = bf16[32,4,34,1,128]{2,0,4,1,3:T(8,128)(2,1)} copy(bf16[32,4,34,1,128]{0,2,4,1,3:T(8,128)(2,1)} %maximum_bitcast_fusion.1) | data formatting | bytes 2228224
  164.4 5.1 pad.4.clone
  169.6 8.7 %copy.394 = bf16[32,4,34,1,8,17]{0,4,5,2,1,3:T(8,128)(2,1)} copy(bf16[32,4,34,1,8,17]{2,0,5,4,1,3:T(8,128)(2,1)} %bitcast.327) | data formatting | bytes 2367488 | tf_op jit(solution)/shard_map/conv_general_dilated | solution.py:47
  179.5 139.8 %fusion.11 = f32[2,32,8,17,2]{2,4,3,1,0:T(2,128)} fusion(bf16[3,3,3,2,32]{4,3,2,1,0:T(2,128)(2,1)S(1)} %copy-done.27, bf16[32,4,34,1,7,2]{0,4,5,2,1,3:T(8,128)(2,1)S(1)} %slice.163, bf16[32,4,34,1,8,17]{0,4,5,2,1,3:T(8,128)(2,1)} %copy.394), kind=kOutput, calls=%fused_computation.11 | convolution fusion | flops 34050048 | bytes 1378688 | tf_op jit(solution)/shard_map/conv_general_dilated | solution.py:47
  325.5 14.1 %all_gather.9 = f32[2,2,256,128]{3,1,0,2:T(2,128)S(1)} all-gather(f32[2,2,32,128]{3,1,0,2:T(2,128)S(1)} %fusion.74), channel_id=1, replica_groups=mesh['slab'=32,'coil'=8] {'coil'}, dimensions={2}, use_global_device_ids=true | all-gather | bytes 589824 | tf_op jit(solution)/shard_map/all_gather | solution.py:123
  350.0 14.7 %all-to-all-start = ((bf16[2,2,2,256,128]{4,1,2,0,3:T(2,128)(2,1)}), bf16[2,2,2,256,128]{4,1,2,0,3:T(2,128)(2,1)S(1)}, u32[]{:S(2)}, u32[]{:S(2)}) async-start(bf16[2,2,2,256,128]{4,1,2,0,3:T(2,128)(2,1)} %copy.404), calls=%async_computation | async-start | bytes 1048576 | tf_op jit(solution)/shard_map/all_to_all | solution.py:99
  369.0 12.5 %all-to-all-done = bf16[2,2,2,256,128]{4,1,2,0,3:T(2,128)(2,1)S(1)} async-done(((bf16[2,2,2,256,128]{4,1,2,0,3:T(2,128)(2,1)}), bf16[2,2,2,256,128]{4,1,2,0,3:T(2,128)(2,1)S(1)}, u32[]{:S(2)}, u32[]{:S(2)}) %all-to-all-start) | async-done | bytes 524320 | tf_op jit(solution)/shard_map/all_to_all | solution.py:99
  385.3 20.3 %all_to_all.162 = bf16[2,2,64,8,128]{4,1,3,0,2:T(2,128)(2,1)S(1)} all-to-all(bf16[2,2,64,8,128]{4,1,3,0,2:T(2,128)(2,1)S(1)} %copy.408), channel_id=1, replica_groups=mesh['slab'=32,'coil'=8] {'slab'}, dimensions={2} | all-to-all | bytes 1048576 | tf_op jit(solution)/shard_map/all_to_all | solution.py:108
  410.0 16.8 %all_to_all.163 = f32[2,2,256,128]{3,1,0,2:T(2,128)} all-to-all(f32[2,2,256,128]{3,1,0,2:T(2,128)} %copy.412), channel_id=1, replica_groups=mesh['slab'=32,'coil'=8] {'coil'}, dimensions={2} | all-to-all | bytes 1048576 | tf_op jit(solution)/shard_map/all_to_all | solution.py:117
  428.1 14.2 %all_gather.10 = f32[2,2,256,128]{3,1,0,2:T(2,128)S(1)} all-gather(f32[2,2,32,128]{3,1,0,2:T(2,128)S(1)} %reduce_sum.146), channel_id=1, replica_groups=mesh['slab'=32,'coil'=8] {'coil'}, dimensions={2}, use_global_device_ids=true | all-gather | bytes 589824 | tf_op jit(solution)/shard_map/all_gather | solution.py:123
  453.8 21.1 %all_to_all.164 = bf16[2,2,2,256,128]{4,1,2,0,3:T(2,128)(2,1)S(1)} all-to-all(bf16[2,2,2,256,128]{4,1,2,0,3:T(2,128)(2,1)} %copy.415), channel_id=1, replica_groups=mesh['slab'=32,'coil'=8] {'slab'}, dimensions={3} | all-to-all | bytes 1048576 | tf_op jit(solution)/shard_map/all_to_all | solution.py:99
  478.3 20.3 %all_to_all.165 = bf16[2,2,64,8,128]{4,1,3,0,2:T(2,128)(2,1)S(1)} all-to-all(bf16[2,2,64,8,128]{4,1,3,0,2:T(2,128)(2,1)S(1)} %copy.419), channel_id=1, replica_groups=mesh['slab'=32,'coil'=8] {'slab'}, dimensions={2} | all-to-all | bytes 1048576 | tf_op jit(solution)/shard_map/all_to_all | solution.py:108
  503.0 16.8 %all_to_all.166 = f32[2,2,256,128]{3,1,0,2:T(2,128)} all-to-all(f32[2,2,256,128]{3,1,0,2:T(2,128)} %copy.423), channel_id=1, replica_groups=mesh['slab'=32,'coil'=8] {'coil'}, dimensions={2} | all-to-all | bytes 1048576 | tf_op jit(solution)/shard_map/all_to_all | solution.py:117
  523.3 19.5 %all_to_all.167 = f32[256,1,2]{2,1,0:T(1,128)} all-to-all(f32[256,1,2]{2,1,0:T(1,128)S(1)} %broadcast_in_dim.15), channel_id=1, replica_groups=mesh['slab'=32,'coil'=8] {'slab','coil'}, dimensions={0} | all-to-all | bytes 4096 | tf_op jit(solution)/shard_map/all_to_all | solution.py:130
  548.7 19.5 %all_to_all.168 = f32[256,1,1]{2,1,0:T(1,128)} all-to-all(f32[256,1,1]{2,1,0:T(1,128)S(1)} %broadcast_in_dim.16), channel_id=1, replica_groups=mesh['slab'=32,'coil'=8] {'slab','coil'}, dimensions={0} | all-to-all | bytes 2048 | tf_op jit(solution)/shard_map/all_to_all | solution.py:130
  572.2 13.6 %all_gather.11 = f32[2,2,256,128]{3,1,0,2:T(2,128)S(1)} all-gather(f32[2,2,32,128]{3,1,0,2:T(2,128)S(1)} %multiply_add_fusion.4), channel_id=1, replica_groups=mesh['slab'=32,'coil'=8] {'coil'}, dimensions={2}, use_global_device_ids=true | all-gather | bytes 589824 | tf_op jit(solution)/shard_map/all_gather | solution.py:123
  597.4 21.0 %all_to_all.169 = bf16[2,2,2,256,128]{4,1,2,0,3:T(2,128)(2,1)S(1)} all-to-all(bf16[2,2,2,256,128]{4,1,2,0,3:T(2,128)(2,1)} %copy.428), channel_id=1, replica_groups=mesh['slab'=32,'coil'=8] {'slab'}, dimensions={3} | all-to-all | bytes 1048576 | tf_op jit(solution)/shard_map/all_to_all | solution.py:99
  621.8 20.3 %all_to_all.170 = bf16[2,2,64,8,128]{4,1,3,0,2:T(2,128)(2,1)S(1)} all-to-all(bf16[2,2,64,8,128]{4,1,3,0,2:T(2,128)(2,1)S(1)} %copy.432), channel_id=1, replica_groups=mesh['slab'=32,'coil'=8] {'slab'}, dimensions={2} | all-to-all | bytes 1048576 | tf_op jit(solution)/shard_map/all_to_all | solution.py:108
  644.0 15.2 %all_to_all.171 = f32[2,2,256,128]{3,1,0,2:T(2,128)S(1)} all-to-all(f32[2,2,256,128]{3,1,0,2:T(2,128)S(1)} %copy.436), channel_id=1, replica_groups=mesh['slab'=32,'coil'=8] {'coil'}, dimensions={2} | all-to-all | bytes 1048576 | tf_op jit(solution)/shard_map/all_to_all | solution.py:117
  661.4 6.5 all-to-all-start.11
  668.3 12.6 %all-to-all-done.11 = f32[256,1,1]{2,1,0:T(1,128)S(1)} async-done(((f32[256,1,1]{2,1,0:T(1,128)}), f32[256,1,1]{2,1,0:T(1,128)S(1)}, u32[]{:S(2)}, u32[]{:S(2)}) %all-to-all-start.11) | async-done | bytes 1056 | tf_op jit(solution)/shard_map/all_to_all | solution.py:130
  (198 shorter events, 169.1 us)
Async XLA Ops:
  0.6 366.3 %copy-start = (f32[2,2,64,8,128]{4,3,2,1,0:T(8,128)S(1)}, f32[2,2,64,8,128]{4,3,2,1,0:T(8,128)}, u32[]{:S(2)}) copy-start(f32[2,2,64,8,128]{4,3,2,1,0:T(8,128)} %param.16) | copy-start | bytes 3145732
  1.6 5.9 collective-permute-start
  5.5 4.5 collective-permute-start.1
  10.0 8.1 %collective-permute-start.2 = (bf16[2,4,1,128]{3,2,1,0:T(2,128)(2,1)S(1)}, bf16[2,4,1,128]{3,2,1,0:T(2,128)(2,1)S(1)}, u32[]{:S(2)}, u32[]{:S(2)}) collective-permute-start(bf16[2,4,1,128]{3,2,1,0:T(2,128)(2,1)S(1)} %get-tuple-element.62), channel_id=1, source_target_pairs={{0,1},{1,2},{2,3},{3,4},{4,5},{5,6},{6,7},{8,9},{9,10},{10,11},{11... | collective-permute-start | bytes 6152 | tf_op jit(solution)/shard_map/ppermute | solution.py:22
  15.2 4.9 collective-permute-start.3
  36.8 10.5 %collective-permute-start.4 = (bf16[32,1,32,128]{3,2,1,0:T(8,128)(2,1)S(1)}, bf16[32,1,32,128]{3,2,1,0:T(8,128)(2,1)}, u32[]{:S(2)}, u32[]{:S(2)}) collective-permute-start(bf16[32,1,32,128]{3,2,1,0:T(8,128)(2,1)S(1)} %copy.380), channel_id=1, source_target_pairs={{0,8},{8,16},{16,24},{24,32},{32,40},{40,48},{48,56},{56,64},{64,7... | collective-permute-start | bytes 786440 | tf_op jit(solution)/shard_map/ppermute | solution.py:22
  44.2 9.1 %collective-permute-start.5 = (bf16[32,1,32,128]{3,2,1,0:T(8,128)(2,1)}, bf16[32,1,32,128]{3,2,1,0:T(8,128)(2,1)}, u32[]{:S(2)}, u32[]{:S(2)}) collective-permute-start(bf16[32,1,32,128]{3,2,1,0:T(8,128)(2,1)} %copy.381), channel_id=1, source_target_pairs={{8,0},{16,8},{24,16},{32,24},{40,32},{48,40},{56,48},{64,56},{72,6... | collective-permute-start | bytes 786440 | tf_op jit(solution)/shard_map/ppermute | solution.py:24
  58.9 7.7 %collective-permute-start.6 = (bf16[32,4,1,128]{0,2,3,1:T(2,128)(2,1)S(1)}, bf16[32,4,1,128]{0,2,3,1:T(2,128)(2,1)S(1)}, u32[]{:S(2)}, u32[]{:S(2)}) collective-permute-start(bf16[32,4,1,128]{0,2,3,1:T(2,128)(2,1)S(1)} %get-tuple-element.28), channel_id=1, source_target_pairs={{0,1},{1,2},{2,3},{3,4},{4,5},{5,6},{6,7},{8,9},{9,10},{10,11},{11... | collective-permute-start | bytes 98312 | tf_op jit(solution)/shard_map/ppermute | solution.py:22
  63.0 7.7 %collective-permute-start.7 = (bf16[32,4,1,128]{0,2,3,1:T(2,128)(2,1)S(1)}, bf16[32,4,1,128]{0,2,3,1:T(2,128)(2,1)S(1)}, u32[]{:S(2)}, u32[]{:S(2)}) collective-permute-start(bf16[32,4,1,128]{0,2,3,1:T(2,128)(2,1)S(1)} %get-tuple-element.29), channel_id=1, source_target_pairs={{1,0},{2,1},{3,2},{4,3},{5,4},{6,5},{7,6},{9,8},{10,9},{11,10},{12... | collective-permute-start | bytes 98312 | tf_op jit(solution)/shard_map/ppermute | solution.py:24
  88.5 19.4 %slice-start = ((s8[4456448]{0:T(1024)(128)(4,1)}), s8[262144]{0:T(1024)(128)(4,1)S(1)}, s32[]{:S(2)}) async-start(s8[4456448]{0:T(1024)(128)(4,1)} %bitcast.324), calls=%async_computation.12 | async-start | bytes 524288
  115.4 11.5 %collective-permute-start.8 = (bf16[32,1,32,128]{3,2,1,0:T(8,128)(2,1)}, bf16[32,1,32,128]{3,2,1,0:T(8,128)(2,1)}, u32[]{:S(2)}, u32[]{:S(2)}) collective-permute-start(bf16[32,1,32,128]{3,2,1,0:T(8,128)(2,1)} %copy.388), channel_id=1, source_target_pairs={{0,8},{8,16},{16,24},{24,32},{32,40},{40,48},{48,56},{56,64},{64,7... | collective-permute-start | bytes 786440 | tf_op jit(solution)/shard_map/ppermute | solution.py:22
  123.2 20.8 %copy-start.11 = (f32[256,1,256]{2,0,1:T(8,128)S(1)}, f32[256,1,256]{2,0,1:T(8,128)}, u32[]{:S(2)}) copy-start(f32[256,1,256]{2,0,1:T(8,128)} %get-tuple-element.70) | copy-start | bytes 786436
  123.2 7.6 %collective-permute-start.9 = (bf16[32,1,32,128]{3,2,1,0:T(8,128)(2,1)}, bf16[32,1,32,128]{3,2,1,0:T(8,128)(2,1)}, u32[]{:S(2)}, u32[]{:S(2)}) collective-permute-start(bf16[32,1,32,128]{3,2,1,0:T(8,128)(2,1)} %copy.389), channel_id=1, source_target_pairs={{8,0},{16,8},{24,16},{32,24},{40,32},{48,40},{56,48},{64,56},{72,6... | collective-permute-start | bytes 786440 | tf_op jit(solution)/shard_map/ppermute | solution.py:24
  137.0 12.9 %collective-permute-start.10 = (bf16[32,4,1,128]{0,2,3,1:T(2,128)(2,1)}, bf16[32,4,1,128]{0,2,3,1:T(2,128)(2,1)}, u32[]{:S(2)}, u32[]{:S(2)}) collective-permute-start(bf16[32,4,1,128]{0,2,3,1:T(2,128)(2,1)} %get-tuple-element.26), channel_id=1, source_target_pairs={{0,1},{1,2},{2,3},{3,4},{4,5},{5,6},{6,7},{8,9},{9,10},{10,11},{11... | collective-permute-start | bytes 98312 | tf_op jit(solution)/shard_map/ppermute | solution.py:22
  142.1 8.0 %collective-permute-start.11 = (bf16[32,4,1,128]{0,2,3,1:T(2,128)(2,1)}, bf16[32,4,1,128]{0,2,3,1:T(2,128)(2,1)}, u32[]{:S(2)}, u32[]{:S(2)}) collective-permute-start(bf16[32,4,1,128]{0,2,3,1:T(2,128)(2,1)} %get-tuple-element.27), channel_id=1, source_target_pairs={{1,0},{2,1},{3,2},{4,3},{5,4},{6,5},{7,6},{9,8},{10,9},{11,10},{12... | collective-permute-start | bytes 98312 | tf_op jit(solution)/shard_map/ppermute | solution.py:24
  319.3 24.9 %copy-start.2 = (f32[2,1,2,256,128]{3,4,1,2,0:T(8,128)S(1)}, f32[2,1,2,256,128]{3,4,1,2,0:T(8,128)}, u32[]{:S(2)}) copy-start(f32[2,1,2,256,128]{3,4,1,2,0:T(8,128)} %copy.490) | copy-start | bytes 1572868
  319.3 24.9 %copy-start.3 = (f32[2,1,2,256,128]{3,4,1,2,0:T(8,128)S(1)}, f32[2,1,2,256,128]{3,4,1,2,0:T(8,128)}, u32[]{:S(2)}) copy-start(f32[2,1,2,256,128]{3,4,1,2,0:T(8,128)} %copy.492) | copy-start | bytes 1572868
  319.3 26.1 %copy-start.8 = (f32[1,256,2,256]{3,1,2,0:T(8,128)S(1)}, f32[1,256,2,256]{3,1,2,0:T(8,128)}, u32[]{:S(2)}) copy-start(f32[1,256,2,256]{3,1,2,0:T(8,128)} %get-tuple-element.46) | copy-start | bytes 1572868
  319.3 26.1 %copy-start.9 = (f32[1,256,2,256]{3,1,2,0:T(8,128)S(1)}, f32[1,256,2,256]{3,1,2,0:T(8,128)}, u32[]{:S(2)}) copy-start(f32[1,256,2,256]{3,1,2,0:T(8,128)} %get-tuple-element.55) | copy-start | bytes 1572868
  325.5 24.5 %copy-start.22 = (f32[2,2,32,128]{3,1,0,2:T(2,128)}, f32[2,2,32,128]{3,1,0,2:T(2,128)S(1)}, u32[]{:S(2)}) copy-start(f32[2,2,32,128]{3,1,0,2:T(2,128)S(1)} %fusion.74) | copy-start | bytes 196612
  340.6 24.1 %copy-start.24 = (s32[64,8]{0,1:T(8,128)S(1)}, s32[64,8]{0,1:T(8,128)}, u32[]{:S(2)}) copy-start(s32[64,8]{0,1:T(8,128)} %param.17) | copy-start | bytes 6148
  350.0 31.4 %all-to-all-start = ((bf16[2,2,2,256,128]{4,1,2,0,3:T(2,128)(2,1)}), bf16[2,2,2,256,128]{4,1,2,0,3:T(2,128)(2,1)S(1)}, u32[]{:S(2)}, u32[]{:S(2)}) async-start(bf16[2,2,2,256,128]{4,1,2,0,3:T(2,128)(2,1)} %copy.404), calls=%async_computation | async-start | bytes 1048576 | tf_op jit(solution)/shard_map/all_to_all | solution.py:99
  366.9 108.2 %copy-start.14 = (f32[1,64,2,64]{3,1,2,0:T(8,128)}, f32[1,64,2,64]{3,1,2,0:T(8,128)S(1)}, u32[]{:S(2)}) copy-start(f32[1,64,2,64]{3,1,2,0:T(8,128)S(1)} %get-tuple-element.57) | copy-start | bytes 98308
  381.5 24.1 %copy-start.6 = (f32[1,256,2,256]{3,1,2,0:T(8,128)S(1)}, f32[1,256,2,256]{3,1,2,0:T(8,128)}, u32[]{:S(2)}) copy-start(f32[1,256,2,256]{3,1,2,0:T(8,128)} %get-tuple-element.47) | copy-start | bytes 1572868
  381.5 24.1 %copy-start.7 = (f32[1,256,2,256]{3,1,2,0:T(8,128)S(1)}, f32[1,256,2,256]{3,1,2,0:T(8,128)}, u32[]{:S(2)}) copy-start(f32[1,256,2,256]{3,1,2,0:T(8,128)} %get-tuple-element.54) | copy-start | bytes 1572868
  453.8 22.8 %copy-start.17 = (f32[1,64,2,64]{3,1,2,0:T(8,128)S(1)}, f32[1,64,2,64]{3,1,2,0:T(8,128)}, u32[]{:S(2)}) copy-start(f32[1,64,2,64]{3,1,2,0:T(8,128)} %get-tuple-element.56) | copy-start | bytes 98308
  453.8 22.8 %copy-start.20 = (f32[1,64,2,64]{3,1,2,0:T(8,128)S(1)}, f32[1,64,2,64]{3,1,2,0:T(8,128)}, u32[]{:S(2)}) copy-start(f32[1,64,2,64]{3,1,2,0:T(8,128)} %get-tuple-element.65) | copy-start | bytes 98308
  521.0 49.0 %copy-start.10 = (f32[2,2,32,128]{3,1,0,2:T(2,128)}, f32[2,2,32,128]{3,1,0,2:T(2,128)S(1)}, u32[]{:S(2)}) copy-start(f32[2,2,32,128]{3,1,0,2:T(2,128)S(1)} %reduce_sum.150) | copy-start | bytes 196612
  597.4 22.7 %copy-start.18 = (f32[1,64,2,64]{3,1,2,0:T(8,128)S(1)}, f32[1,64,2,64]{3,1,2,0:T(8,128)}, u32[]{:S(2)}) copy-start(f32[1,64,2,64]{3,1,2,0:T(8,128)} %get-tuple-element.56) | copy-start | bytes 98308
  597.4 22.7 %copy-start.21 = (f32[1,64,2,64]{3,1,2,0:T(8,128)S(1)}, f32[1,64,2,64]{3,1,2,0:T(8,128)}, u32[]{:S(2)}) copy-start(f32[1,64,2,64]{3,1,2,0:T(8,128)} %get-tuple-element.65) | copy-start | bytes 98308
  643.4 39.7 %copy-start.23 = (f32[2,2,32,128]{3,1,0,2:T(2,128)S(1)}, f32[2,2,32,128]{3,1,0,2:T(2,128)}, u32[]{:S(2)}) copy-start(f32[2,2,32,128]{3,1,0,2:T(2,128)} %copy-done.22) | copy-start | bytes 196612
  661.4 19.5 %all-to-all-start.11 = ((f32[256,1,1]{2,1,0:T(1,128)}), f32[256,1,1]{2,1,0:T(1,128)S(1)}, u32[]{:S(2)}, u32[]{:S(2)}) async-start(f32[256,1,1]{2,1,0:T(1,128)} %broadcast_in_dim.17), calls=%async_computation.11 | async-start | bytes 262144 | tf_op jit(solution)/shard_map/all_to_all | solution.py:130
  (12 other events, 111.1 us)
where the time goes:
time: 697 us; the launch traced here: 685 us
  blocking collectives  233 us (33%)
  matrix products  181 us (26%)
  local copies, waits for them, and re-layouts  123 us (18%)
  starting transfers between devices  57.9 us (8%)
  other arithmetic  46.4 us (7%)
  waiting for transfers between devices  36.7 us (5%)
    conv_general_dilated x3, matrix products, conv_layer(): lax.conv_general_dilated(padded[None], kernel, (1, 1, 1), ((0, 0), (0, 0)...  156 us
    all_to_all x3, blocking collectives, coil_term(): lax.all_to_all(back.astype(jnp.bfloat16), 'slab', split_axis=2, concat_ax...  60.9 us
    all_to_all x3, blocking collectives, combine_coils(): lax.all_to_all(partial_value, 'coil', split_axis=2, concat_axis=0, tiled=...  48.8 us
    all_to_all x2, blocking collectives, coil_term(): lax.all_to_all(spectrum.astype(jnp.bfloat16), 'slab', split_axis=3, conca...  42.1 us
    all_gather x3, blocking collectives, gather_rows(): return lax.all_gather(value, 'coil', axis=2, tiled=True)  42 us
    all_to_all x2, blocking collectives, global_sums(): lax.all_to_all(spread, axes, split_axis=0, concat_axis=0, tiled=True)  39 us
    ppermute x6, starting transfers between devices, extended(): lax.ppermute(tail, axis, [(i, (i + 1) % count) for i in range(ends)])  27 us
    conv_general_dilated x9, local copies, waits for them, and re-layouts, conv_layer(): lax.conv_general_dilated(padded[None], kernel, (1, 1, 1), ((0, 0), (0, 0)...  26 us
  transfers between devices with their start and end apart: 14, of which 8 were waited for; matrix products, arithmetic and copies ran while one was open for 4% of the time, Pallas kernels for 0%

commit v1 on v0

--- a/solution.py
+++ b/solution.py
@@ -9,6 +9,24 @@
 STRIDE = 20
 REG_WEIGHT = 0.5
 HIGHEST_PRECISION = lax.Precision.HIGHEST
+
+
+def collect(value, axis, dim):
+    ways, here, lap = (lax.axis_size(axis), lax.axis_index(axis), value.shape[dim])
+    dims = [n * ways if d == dim else n for d, n in enumerate(value.shape)]
+    full = lax.dynamic_update_slice_in_dim(
+        jnp.zeros(dims, value.dtype), value, here * lap, axis=dim
+    )
+    going_up = going_down = value
+    for far in range(1, ways // 2 + 1):
+        going_up = lax.ppermute(going_up, axis, [(d, (d + 1) % ways) for d in range(ways)])
+        full = lax.dynamic_update_slice_in_dim(full, going_up, (here - far) % ways * lap, axis=dim)
+        if 2 * far < ways:
+            going_down = lax.ppermute(going_down, axis, [(d, (d - 1) % ways) for d in range(ways)])
+            full = lax.dynamic_update_slice_in_dim(
+                full, going_down, (here + far) % ways * lap, axis=dim
+            )
+    return full
 
 
 def extended(cells, sides, width):
@@ -120,7 +138,7 @@
 
 
 def gather_rows(value):
-    return lax.all_gather(value, "coil", axis=2, tiled=True)
+    return collect(value, "coil", 2)
 
 
 def global_sums(values):

time: 697 us -> 788 us (1.13)
  local copies, waits for them, and re-layouts: 123 us -> 203 us
  blocking collectives: 233 us -> 194 us
  starting transfers between devices: 57.9 us -> 92.8 us
  waiting for transfers between devices: 36.7 us -> 56.2 us
    dynamic_update_slice x0 -> x24, local copies, waits for them, and re-layouts: none -> 55.4 us  [the longest x12 25.9 us: collect(): lax.dynamic_update_slice_in_dim(full, going_up, (here - far) % ways * lap...]
    all_gather x3 -> x0, blocking collectives: 42 us -> none  [gather_rows(): return lax.all_gather(value, 'coil', axis=2, tiled=True)]
    ppermute x0 -> x21, local copies, waits for them, and re-layouts: none -> 34.8 us  [the longest x12 19.5 us: collect(): lax.ppermute(going_up, axis, [(d, (d + 1) % ways) for d in range(ways)])]
    ppermute x0 -> x21, starting transfers between devices: none -> 22.5 us  [the longest x12 16.8 us: collect(): lax.ppermute(going_up, axis, [(d, (d + 1) % ways) for d in range(ways)])]
    all_to_all x3, blocking collectives: 48.8 us -> 62.1 us  [combine_coils(): lax.all_to_all(partial_value, 'coil', split_axis=2, concat_axis=0, tiled=...]
    ppermute x6, starting transfers between devices: 27 us -> 38 us  [extended(): lax.ppermute(tail, axis, [(i, (i + 1) % count) for i in range(ends)])]
    mul x9 -> x3, local copies, waits for them, and re-layouts: 13.6 us -> 3.19 us  [times_sens(): real_part = sens[:, 0] * image[0] - sens[:, 1] * image[1]]
    ppermute x6, waiting for transfers between devices: 11.5 us -> 20.1 us  [extended(): lax.ppermute(head, axis, [((i + 1) % count, i) for i in range(ends)])]
  transfers between devices with their start and end apart: 14 -> 35, of which waited for: 8 -> 22; matrix products, arithmetic and copies ran while one was open for 4% -> 14% of each run, Pallas kernels for 0% -> 0%
where the time goes in v1:
time: 788 us; the launch traced here: 775 us
  local copies, waits for them, and re-layouts  203 us (26%)
  blocking collectives  194 us (25%)
  matrix products  182 us (23%)
  starting transfers between devices  92.8 us (12%)
  waiting for transfers between devices  56.2 us (7%)
  other arithmetic  39.9 us (5%)
    conv_general_dilated x3, matrix products, conv_layer(): lax.conv_general_dilated(padded[None], kernel, (1, 1, 1), ((0, 0), (0, 0)...  155 us
    all_to_all x3, blocking collectives, combine_coils(): lax.all_to_all(partial_value, 'coil', split_axis=2, concat_axis=0, tiled=...  62.1 us
    all_to_all x3, blocking collectives, coil_term(): lax.all_to_all(back.astype(jnp.bfloat16), 'slab', split_axis=2, concat_ax...  57.8 us
    all_to_all x2, blocking collectives, global_sums(): lax.all_to_all(spread, axes, split_axis=0, concat_axis=0, tiled=True)  39.8 us
    ppermute x6, starting transfers between devices, extended(): lax.ppermute(tail, axis, [(i, (i + 1) % count) for i in range(ends)])  38 us
    all_to_all x2, blocking collectives, coil_term(): lax.all_to_all(spectrum.astype(jnp.bfloat16), 'slab', split_axis=3, conca...  34.8 us
    dynamic_update_slice x12, local copies, waits for them, and re-layouts, collect(): lax.dynamic_update_slice_in_dim(full, going_up, (here - far) % ways * lap...  25.9 us
    conv_general_dilated x9, local copies, waits for them, and re-layouts, conv_layer(): lax.conv_general_dilated(padded[None], kernel, (1, 1, 1), ((0, 0), (0, 0)...  24.3 us
  transfers between devices with their start and end apart: 35, of which 22 were waited for; matrix products, arithmetic and copies ran while one was open for 14% of the time, Pallas kernels for 0%

profile of v1, /device:TPU:1, one launch (start us, length us, event | category | flops | bytes accessed | tf_op | source)
XLA Modules:
  0.0 774.8 jit_solution(18273814597511565372)
XLA Ops:
  10.0 5.2 collective-permute-start.2
  22.7 7.8 %broadcast_select_fusion.1 = f32[2,32,8,17,32]{4,2,3,1,0:T(8,128)S(1)} fusion(pred[8,17]{0,1:T(8,128)(4,1)} %constant.200, bf16[3,3,3,32,2]{3,4,2,1,0:T(2,128)(2,1)} %param.11, bf16[2,4,34,1,7,2]{4,0,5,2,1,3:T(2,128)(2,1)S(1)} %slice.155, bf16[2,4,34,1,8,17]{4,0,5,2,1,3:T(2,128)(2,1)S(1)} %copy.504), kind=kOutput, calls=%fused_computation.23 | convolution fusion | flops 30607616 | bytes 1199304 | tf_op jit(solution)/shard_map/conv_general_dilated | solution.py:65
  36.8 14.9 %collective-permute-start.4 = (bf16[32,1,32,128]{3,2,1,0:T(8,128)(2,1)S(1)}, bf16[32,1,32,128]{3,2,1,0:T(8,128)(2,1)}, u32[]{:S(2)}, u32[]{:S(2)}) collective-permute-start(bf16[32,1,32,128]{3,2,1,0:T(8,128)(2,1)S(1)} %copy.506), channel_id=1, source_target_pairs={{0,8},{8,16},{16,24},{24,32},{32,40},{40,48},{48,56},{56,64},{64,7... | collective-permute-start | bytes 786440 | tf_op jit(solution)/shard_map/ppermute | solution.py:40
  60.0 4.2 collective-permute-done.5
  77.1 4.4 collective-permute-done.7
  81.5 4.7 maximum_bitcast_fusion
  86.2 8.1 %copy.641 = bf16[32,4,34,1,128]{2,0,4,1,3:T(8,128)(2,1)} copy(bf16[32,4,34,1,128]{0,2,4,1,3:T(8,128)(2,1)} %maximum_bitcast_fusion) | data formatting | bytes 2228224
  94.3 5.2 pad.2.clone
  99.5 8.8 %copy.512 = bf16[32,4,34,1,8,17]{0,4,5,2,1,3:T(8,128)(2,1)} copy(bf16[32,4,34,1,8,17]{2,0,5,4,1,3:T(8,128)(2,1)} %bitcast.328) | data formatting | bytes 2367488 | tf_op jit(solution)/shard_map/conv_general_dilated | solution.py:65
  109.5 8.6 %broadcast_select_fusion = f32[2,32,8,17,32]{4,2,3,1,0:T(8,128)S(1)} fusion(pred[8,17]{0,1:T(8,128)(4,1)S(1)} %copy-done.25, bf16[3,3,3,32,32]{4,3,2,1,0:T(8,128)(2,1)S(1)} %copy-done.26, bf16[32,4,34,1,7,2]{0,4,5,2,1,3:T(8,128)(2,1)S(1)} %slice.159, bf16[32,4,34,1,8,17]{0,4,5,2,1,3:T(8,128)(2,1)} %copy.512), kind=kOutput, calls=%fused_computation.22 | convolution fusion | flops 485543936 | bytes 2475144 | tf_op jit(solution)/shard_map/conv_general_dilated | solution.py:65
  125.9 4.8 collective-permute-start.8
  147.6 5.1 collective-permute-start.10
  156.3 4.4 collective-permute-done.11
  160.7 6.3 maximum_bitcast_fusion.1
  167.0 8.1 %copy.642 = bf16[32,4,34,1,128]{2,0,4,1,3:T(8,128)(2,1)} copy(bf16[32,4,34,1,128]{0,2,4,1,3:T(8,128)(2,1)} %maximum_bitcast_fusion.1) | data formatting | bytes 2228224
  175.1 5.1 pad.4.clone
  180.3 8.7 %copy.520 = bf16[32,4,34,1,8,17]{0,4,5,2,1,3:T(8,128)(2,1)} copy(bf16[32,4,34,1,8,17]{2,0,5,4,1,3:T(8,128)(2,1)} %bitcast.327) | data formatting | bytes 2367488 | tf_op jit(solution)/shard_map/conv_general_dilated | solution.py:65
  190.2 139.0 %fusion.11 = f32[2,32,8,17,2]{2,4,3,1,0:T(2,128)S(1)} fusion(bf16[3,3,3,2,32]{4,3,2,1,0:T(2,128)(2,1)S(1)} %copy-done.27, bf16[32,4,34,1,7,2]{0,4,5,2,1,3:T(8,128)(2,1)S(1)} %slice.163, bf16[32,4,34,1,8,17]{0,4,5,2,1,3:T(8,128)(2,1)} %copy.520), kind=kOutput, calls=%fused_computation.11 | convolution fusion | flops 34050048 | bytes 1378688 | tf_op jit(solution)/shard_map/conv_general_dilated | solution.py:65
  382.8 15.3 %all-to-all-start = ((bf16[2,2,2,256,128]{4,1,2,0,3:T(2,128)(2,1)}), bf16[2,2,2,256,128]{4,1,2,0,3:T(2,128)(2,1)}, u32[]{:S(2)}, u32[]{:S(2)}) async-start(bf16[2,2,2,256,128]{4,1,2,0,3:T(2,128)(2,1)} %copy.536), calls=%async_computation | async-start | bytes 1048576 | tf_op jit(solution)/shard_map/all_to_all | solution.py:117
  402.3 12.5 %all-to-all-done = bf16[2,2,2,256,128]{4,1,2,0,3:T(2,128)(2,1)} async-done(((bf16[2,2,2,256,128]{4,1,2,0,3:T(2,128)(2,1)}), bf16[2,2,2,256,128]{4,1,2,0,3:T(2,128)(2,1)}, u32[]{:S(2)}, u32[]{:S(2)}) %all-to-all-start) | async-done | bytes 524320 | tf_op jit(solution)/shard_map/all_to_all | solution.py:117
  419.6 20.3 %all_to_all.162 = bf16[2,2,64,8,128]{4,1,3,0,2:T(2,128)(2,1)S(1)} all-to-all(bf16[2,2,64,8,128]{4,1,3,0,2:T(2,128)(2,1)S(1)} %copy.540), channel_id=1, replica_groups=mesh['slab'=32,'coil'=8] {'slab'}, dimensions={2} | all-to-all | bytes 1048576 | tf_op jit(solution)/shard_map/all_to_all | solution.py:126
  444.3 16.8 %all_to_all.167 = f32[2,2,256,128]{3,1,0,2:T(2,128)} all-to-all(f32[2,2,256,128]{3,1,0,2:T(2,128)} %copy.544), channel_id=1, replica_groups=mesh['slab'=32,'coil'=8] {'coil'}, dimensions={2} | all-to-all | bytes 1048576 | tf_op jit(solution)/shard_map/all_to_all | solution.py:135
  513.9 17.5 %all_to_all.163 = bf16[2,2,2,256,128]{4,1,2,0,3:T(2,128)(2,1)S(1)} all-to-all(bf16[2,2,2,256,128]{4,1,2,0,3:T(2,128)(2,1)} %copy.553), channel_id=1, replica_groups=mesh['slab'=32,'coil'=8] {'slab'}, dimensions={3} | all-to-all | bytes 1048576 | tf_op jit(solution)/shard_map/all_to_all | solution.py:117
  534.8 18.7 %all_to_all.164 = bf16[2,2,64,8,128]{4,1,3,0,2:T(2,128)(2,1)S(1)} all-to-all(bf16[2,2,64,8,128]{4,1,3,0,2:T(2,128)(2,1)S(1)} %copy.557), channel_id=1, replica_groups=mesh['slab'=32,'coil'=8] {'slab'}, dimensions={2} | all-to-all | bytes 1048576 | tf_op jit(solution)/shard_map/all_to_all | solution.py:126
  558.0 22.7 %all_to_all.168 = f32[2,2,256,128]{3,1,0,2:T(2,128)} all-to-all(f32[2,2,256,128]{3,1,0,2:T(2,128)} %copy.561), channel_id=1, replica_groups=mesh['slab'=32,'coil'=8] {'coil'}, dimensions={2} | all-to-all | bytes 1048576 | tf_op jit(solution)/shard_map/all_to_all | solution.py:135
  584.0 20.2 %all_to_all.169 = f32[256,1,2]{2,1,0:T(1,128)} all-to-all(f32[256,1,2]{2,1,0:T(1,128)S(1)} %broadcast_in_dim.15), channel_id=1, replica_groups=mesh['slab'=32,'coil'=8] {'slab','coil'}, dimensions={0} | all-to-all | bytes 4096 | tf_op jit(solution)/shard_map/all_to_all | solution.py:148
  609.5 19.6 %all_to_all.170 = f32[256,1,1]{2,1,0:T(1,128)} all-to-all(f32[256,1,1]{2,1,0:T(1,128)S(1)} %broadcast_in_dim.16), channel_id=1, replica_groups=mesh['slab'=32,'coil'=8] {'slab','coil'}, dimensions={0} | all-to-all | bytes 2048 | tf_op jit(solution)/shard_map/all_to_all | solution.py:148
  684.4 17.2 %all_to_all.165 = bf16[2,2,2,256,128]{4,1,2,0,3:T(2,128)(2,1)S(1)} all-to-all(bf16[2,2,2,256,128]{4,1,2,0,3:T(2,128)(2,1)} %copy.572), channel_id=1, replica_groups=mesh['slab'=32,'coil'=8] {'slab'}, dimensions={3} | all-to-all | bytes 1048576 | tf_op jit(solution)/shard_map/all_to_all | solution.py:117
  705.0 18.7 %all_to_all.166 = bf16[2,2,64,8,128]{4,1,3,0,2:T(2,128)(2,1)S(1)} all-to-all(bf16[2,2,64,8,128]{4,1,3,0,2:T(2,128)(2,1)S(1)} %copy.576), channel_id=1, replica_groups=mesh['slab'=32,'coil'=8] {'slab'}, dimensions={2} | all-to-all | bytes 1048576 | tf_op jit(solution)/shard_map/all_to_all | solution.py:126
  725.6 22.6 %all_to_all.171 = f32[2,2,256,128]{3,1,0,2:T(2,128)S(1)} all-to-all(f32[2,2,256,128]{3,1,0,2:T(2,128)S(1)} %copy.580), channel_id=1, replica_groups=mesh['slab'=32,'coil'=8] {'coil'}, dimensions={2} | all-to-all | bytes 1048576 | tf_op jit(solution)/shard_map/all_to_all | solution.py:135
  750.4 7.4 all-to-all-start.11
  758.1 12.6 %all-to-all-done.11 = f32[256,1,1]{2,1,0:T(1,128)S(1)} async-done(((f32[256,1,1]{2,1,0:T(1,128)}), f32[256,1,1]{2,1,0:T(1,128)S(1)}, u32[]{:S(2)}, u32[]{:S(2)}) %all-to-all-start.11) | async-done | bytes 1056 | tf_op jit(solution)/shard_map/all_to_all | solution.py:148
  (282 shorter events, 272.6 us)
Async XLA Ops:
  1.6 5.9 collective-permute-start
  5.5 4.5 collective-permute-start.1
  10.0 8.1 %collective-permute-start.2 = (bf16[2,4,1,128]{3,2,1,0:T(2,128)(2,1)S(1)}, bf16[2,4,1,128]{3,2,1,0:T(2,128)(2,1)S(1)}, u32[]{:S(2)}, u32[]{:S(2)}) collective-permute-start(bf16[2,4,1,128]{3,2,1,0:T(2,128)(2,1)S(1)} %get-tuple-element.62), channel_id=1, source_target_pairs={{0,1},{1,2},{2,3},{3,4},{4,5},{5,6},{6,7},{8,9},{9,10},{10,11},{11... | collective-permute-start | bytes 6152 | tf_op jit(solution)/shard_map/ppermute | solution.py:40
  15.2 4.9 collective-permute-start.3
  36.8 19.5 %collective-permute-start.4 = (bf16[32,1,32,128]{3,2,1,0:T(8,128)(2,1)S(1)}, bf16[32,1,32,128]{3,2,1,0:T(8,128)(2,1)}, u32[]{:S(2)}, u32[]{:S(2)}) collective-permute-start(bf16[32,1,32,128]{3,2,1,0:T(8,128)(2,1)S(1)} %copy.506), channel_id=1, source_target_pairs={{0,8},{8,16},{16,24},{24,32},{32,40},{40,48},{48,56},{56,64},{64,7... | collective-permute-start | bytes 786440 | tf_op jit(solution)/shard_map/ppermute | solution.py:40
  55.1 9.1 %collective-permute-start.5 = (bf16[32,1,32,128]{3,2,1,0:T(8,128)(2,1)}, bf16[32,1,32,128]{3,2,1,0:T(8,128)(2,1)}, u32[]{:S(2)}, u32[]{:S(2)}) collective-permute-start(bf16[32,1,32,128]{3,2,1,0:T(8,128)(2,1)} %copy.507), channel_id=1, source_target_pairs={{8,0},{16,8},{24,16},{32,24},{40,32},{48,40},{56,48},{64,56},{72,6... | collective-permute-start | bytes 786440 | tf_op jit(solution)/shard_map/ppermute | solution.py:42
  69.7 7.4 collective-permute-start.6
  73.8 7.7 collective-permute-start.7
  125.9 9.4 %collective-permute-start.8 = (bf16[32,1,32,128]{3,2,1,0:T(8,128)(2,1)S(1)}, bf16[32,1,32,128]{3,2,1,0:T(8,128)(2,1)}, u32[]{:S(2)}, u32[]{:S(2)}) collective-permute-start(bf16[32,1,32,128]{3,2,1,0:T(8,128)(2,1)S(1)} %copy.514), channel_id=1, source_target_pairs={{0,8},{8,16},{16,24},{24,32},{32,40},{40,48},{48,56},{56,64},{64,7... | collective-permute-start | bytes 786440 | tf_op jit(solution)/shard_map/ppermute | solution.py:40
  134.0 7.4 collective-permute-start.9
  147.6 8.7 %collective-permute-start.10 = (bf16[32,4,1,128]{0,2,3,1:T(2,128)(2,1)}, bf16[32,4,1,128]{0,2,3,1:T(2,128)(2,1)S(1)}, u32[]{:S(2)}, u32[]{:S(2)}) collective-permute-start(bf16[32,4,1,128]{0,2,3,1:T(2,128)(2,1)} %get-tuple-element.26), channel_id=1, source_target_pairs={{0,1},{1,2},{2,3},{3,4},{4,5},{5,6},{6,7},{8,9},{9,10},{10,11},{11... | collective-permute-start | bytes 98312 | tf_op jit(solution)/shard_map/ppermute | solution.py:40
  152.7 8.0 %collective-permute-start.11 = (bf16[32,4,1,128]{0,2,3,1:T(2,128)(2,1)}, bf16[32,4,1,128]{0,2,3,1:T(2,128)(2,1)}, u32[]{:S(2)}, u32[]{:S(2)}) collective-permute-start(bf16[32,4,1,128]{0,2,3,1:T(2,128)(2,1)} %get-tuple-element.27), channel_id=1, source_target_pairs={{1,0},{2,1},{3,2},{4,3},{5,4},{6,5},{7,6},{9,8},{10,9},{11,10},{12... | collective-permute-start | bytes 98312 | tf_op jit(solution)/shard_map/ppermute | solution.py:42
  332.3 3.9 collective-permute-start.13
  332.8 3.4 collective-permute-start.14
  336.2 3.8 collective-permute-start.15
  336.3 3.8 collective-permute-start.16
  340.0 28.3 %collective-permute-start.17 = (f32[2,2,32,128]{3,1,0,2:T(2,128)}, f32[2,2,32,128]{3,1,0,2:T(2,128)}, u32[]{:S(2)}, u32[]{:S(2)}) collective-permute-start(f32[2,2,32,128]{3,1,0,2:T(2,128)} %collective-permute-done.15), channel_id=1, source_target_pairs={{0,7},{1,0},{2,1},{3,2},{4,3},{5,4},{6,5},{7,6},{8,15},{9,8},{10,9... | collective-permute-start | bytes 196616 | tf_op jit(solution)/shard_map/ppermute | solution.py:25
  340.0 31.8 %collective-permute-start.18 = (f32[2,2,32,128]{3,1,0,2:T(2,128)}, f32[2,2,32,128]{3,1,0,2:T(2,128)}, u32[]{:S(2)}, u32[]{:S(2)}) collective-permute-start(f32[2,2,32,128]{3,1,0,2:T(2,128)} %collective-permute-done.16), channel_id=1, source_target_pairs={{0,1},{1,2},{2,3},{3,4},{4,5},{5,6},{6,7},{7,0},{8,9},{9,10},{10,1... | collective-permute-start | bytes 196616 | tf_op jit(solution)/shard_map/ppermute | solution.py:22
  382.8 32.0 %all-to-all-start = ((bf16[2,2,2,256,128]{4,1,2,0,3:T(2,128)(2,1)}), bf16[2,2,2,256,128]{4,1,2,0,3:T(2,128)(2,1)}, u32[]{:S(2)}, u32[]{:S(2)}) async-start(bf16[2,2,2,256,128]{4,1,2,0,3:T(2,128)(2,1)} %copy.536), calls=%async_computation | async-start | bytes 1048576 | tf_op jit(solution)/shard_map/all_to_all | solution.py:117
  463.6 4.0 collective-permute-start.20
  464.9 4.1 collective-permute-start.21
  468.2 4.0 collective-permute-start.22
  469.0 5.0 collective-permute-start.23
  472.2 27.2 %collective-permute-start.24 = (f32[2,2,32,128]{3,1,0,2:T(2,128)}, f32[2,2,32,128]{3,1,0,2:T(2,128)}, u32[]{:S(2)}, u32[]{:S(2)}) collective-permute-start(f32[2,2,32,128]{3,1,0,2:T(2,128)} %collective-permute-done.22), channel_id=1, source_target_pairs={{0,7},{1,0},{2,1},{3,2},{4,3},{5,4},{6,5},{7,6},{8,15},{9,8},{10,9... | collective-permute-start | bytes 196616 | tf_op jit(solution)/shard_map/ppermute | solution.py:25
  474.1 28.8 %collective-permute-start.25 = (f32[2,2,32,128]{3,1,0,2:T(2,128)}, f32[2,2,32,128]{3,1,0,2:T(2,128)}, u32[]{:S(2)}, u32[]{:S(2)}) collective-permute-start(f32[2,2,32,128]{3,1,0,2:T(2,128)} %collective-permute-done.23), channel_id=1, source_target_pairs={{0,1},{1,2},{2,3},{3,4},{4,5},{5,6},{6,7},{7,0},{8,9},{9,10},{10,1... | collective-permute-start | bytes 196616 | tf_op jit(solution)/shard_map/ppermute | solution.py:22
  634.0 4.0 collective-permute-start.27
  635.3 4.2 collective-permute-start.28
  638.6 3.8 collective-permute-start.29
  639.6 5.0 collective-permute-start.30
  642.4 27.4 %collective-permute-start.31 = (f32[2,2,32,128]{3,1,0,2:T(2,128)}, f32[2,2,32,128]{3,1,0,2:T(2,128)}, u32[]{:S(2)}, u32[]{:S(2)}) collective-permute-start(f32[2,2,32,128]{3,1,0,2:T(2,128)} %collective-permute-done.29), channel_id=1, source_target_pairs={{0,7},{1,0},{2,1},{3,2},{4,3},{5,4},{6,5},{7,6},{8,15},{9,8},{10,9... | collective-permute-start | bytes 196616 | tf_op jit(solution)/shard_map/ppermute | solution.py:25
  644.6 28.7 %collective-permute-start.32 = (f32[2,2,32,128]{3,1,0,2:T(2,128)}, f32[2,2,32,128]{3,1,0,2:T(2,128)}, u32[]{:S(2)}, u32[]{:S(2)}) collective-permute-start(f32[2,2,32,128]{3,1,0,2:T(2,128)} %collective-permute-done.30), channel_id=1, source_target_pairs={{0,1},{1,2},{2,3},{3,4},{4,5},{5,6},{6,7},{7,0},{8,9},{9,10},{10,1... | collective-permute-start | bytes 196616 | tf_op jit(solution)/shard_map/ppermute | solution.py:22
  750.4 20.4 %all-to-all-start.11 = ((f32[256,1,1]{2,1,0:T(1,128)}), f32[256,1,1]{2,1,0:T(1,128)S(1)}, u32[]{:S(2)}, u32[]{:S(2)}) async-start(f32[256,1,1]{2,1,0:T(1,128)} %broadcast_in_dim.17), calls=%async_computation.11 | async-start | bytes 262144 | tf_op jit(solution)/shard_map/all_to_all | solution.py:148
  (33 other events, 1043.0 us)
